TPU v7x, 512 devices: a whole 4x8x8 slice. The times are simulated.
512 devices in a mesh: expert: 64 (over x, z, core), group: 8 (over y).
Axes of the slice: x: 4, y: 8, z: 8, core: 2. Of those that a mesh axis runs over, the one named last changes fastest.
Arguments:
- tokens: bfloat16 [4096, 4096], P('expert', 'group'), may hold values from -6 to 6
- gate_weight: bfloat16 [64, 1536, 4096], P('expert', 'group'), may hold values from -0.09375 to 0.09375
- up_weight: bfloat16 [64, 1536, 4096], P('expert', 'group'), may hold values from -0.09375 to 0.09375
- down_weight: bfloat16 [64, 1536, 4096], P('expert', 'group'), may hold values from -0.15625 to 0.15625
- expert_ids: int32 [4096, 8], P('expert'), may hold values from 0 to 63, all different within a row; in each aligned block of 64 rows (0 to 63, 64 to 127, ...) at most 12 rows name the same one
- gate_scores: bfloat16 [4096, 8], P('expert'), may hold values from 0.19921875 to 1
Outputs:
- mixed: bfloat16 [4096, 4096], P('expert', 'group')
Inputs may be any that keep to these rules, and one draw needn't show every extreme that they name: `expert_ids`: the 8 experts of a token are distinct; within the 64 rows of one device no expert is named by more than 12 rows, a bound that some block reaches.
All inputs are finite; a program needn't handle non-finite values.
Results may differ from a plain program's by a relative error of at most 0.019.
Values may be sent and summed in bfloat16 or wider, within the bound.
No kernel may reach another device: no remote copies, remote signals or barrier semaphores. Data moves between devices by JAX's collectives and lax.ppermute only.
A program may use at most 128 MiB of HBM per device.

v0:
```python
import jax
import jax.numpy as jnp
from jax import lax
from jax.sharding import PartitionSpec as P


def per_device(tokens, gate_weight, up_weight, down_weight, expert_ids, gate_scores):
    experts = lax.axis_size("expert")
    tok_rows = tokens.shape[0]
    top_count = expert_ids.shape[1]
    capacity = tok_rows * top_count * 3 // (2 * experts)
    flat_ids = expert_ids.reshape(-1)
    onehot = (flat_ids[:, None] == jnp.arange(experts, dtype=jnp.int32)[None, :]).astype(jnp.int32)
    before = jnp.cumsum(onehot, axis=0) - onehot
    slot_index = jnp.sum(before * onehot, axis=1).reshape(tok_rows, top_count)
    slot_keys = expert_ids * capacity + slot_index
    columns = jnp.arange(experts * capacity, dtype=jnp.int32)
    matches = slot_keys[:, :, None] == columns[None, None, :]
    selector = jnp.any(matches, axis=1).astype(jnp.bfloat16)
    weights = jnp.sum(
        jnp.where(matches, gate_scores[:, :, None].astype(jnp.float32), 0.0), axis=1
    ).astype(jnp.bfloat16)
    whole_rows = lax.all_gather(tokens, "group", axis=1, tiled=True)
    placed = lax.dot_general(
        selector, whole_rows, (((0,), (0,)), ((), ())), preferred_element_type=jnp.float32
    )
    arrived = lax.all_to_all(
        placed.astype(jnp.bfloat16).reshape(experts, capacity, whole_rows.shape[1]),
        "expert",
        split_axis=0,
        concat_axis=0,
        tiled=True,
    )
    row_block = arrived.reshape(-1, arrived.shape[2])
    gate_value = lax.dot_general(
        row_block, gate_weight[0], (((1,), (1,)), ((), ())), preferred_element_type=jnp.float32
    )
    up_value = lax.dot_general(
        row_block, up_weight[0], (((1,), (1,)), ((), ())), preferred_element_type=jnp.float32
    )
    hidden = (jax.nn.silu(gate_value) * up_value).astype(jnp.bfloat16)
    partial_value = jnp.dot(hidden, down_weight[0], preferred_element_type=jnp.float32)
    returned = lax.all_to_all(
        partial_value.astype(jnp.bfloat16).reshape(arrived.shape),
        "expert",
        split_axis=0,
        concat_axis=0,
        tiled=True,
    )
    combined = jnp.dot(
        weights, returned.reshape(experts * capacity, -1), preferred_element_type=jnp.float32
    )
    return lax.psum_scatter(combined.astype(jnp.bfloat16), "group", scatter_dimension=1, tiled=True)


def solution(mesh):
    placed = (
        P("expert", "group"),
        P("expert", "group", None),
        P("expert", "group", None),
        P("expert", "group", None),
        P("expert", None),
        P("expert", None),
    )
    return jax.shard_map(
        per_device, mesh=mesh, in_specs=placed, out_specs=P("expert", "group"), check_vma=False
    )
```

profile of v0, /device:TPU:2, one launch (start us, length us, event | category | flops | bytes accessed | tf_op | source)
XLA Modules:
  0.0 540.2 jit_solution(18164312794375199998)
XLA Ops:
  6.5 0.9 copy.21
  7.4 0.1 eq.42
  7.5 0.1 eq.38
  7.6 1.2 reduce-window.6
  8.8 0.2 slice_reduce_fusion
  9.1 0.1 fusion.22
  9.2 0.1 reshape.36
  9.4 0.7 multiply_add_fusion
  10.2 0.5 fusion.5
  10.7 27.1 %all_gather.3 = bf16[64,4096]{1,0:T(8,128)(2,1)S(1)} all-gather(bf16[64,512]{1,0:T(8,128)(2,1)} %param.6), channel_id=1, replica_groups=mesh['expert'=64,'group'=8] {'group'}, dimensions={1}, use_global_device_ids=true | all-gather | bytes 589824 | tf_op jit(solution)/shard_map/all_gather | solution.py:23
  37.9 4.6 convolution_convert_fusion
  42.4 9.8 %reshape.37 = bf16[64,12,4096]{2,1,0:T(8,128)(2,1)} reshape(bf16[768,4096]{1,0:T(8,128)(2,1)} %convolution_convert_fusion) | data formatting | bytes 12582912 | tf_op jit(solution)/shard_map/reshape | solution.py:28
  52.2 198.1 %all_to_all.10 = bf16[64,12,4096]{2,1,0:T(8,128)(2,1)} all-to-all(bf16[64,12,4096]{2,1,0:T(8,128)(2,1)} %reshape.37), channel_id=1, replica_groups=mesh['expert'=64,'group'=8] {'expert'}, dimensions={0} | all-to-all | bytes 12582912 | tf_op jit(solution)/shard_map/all_to_all | solution.py:27
  250.3 10.1 %reshape.38 = bf16[768,4096]{1,0:T(8,128)(2,1)} reshape(bf16[64,12,4096]{2,1,0:T(8,128)(2,1)} %all_to_all.10) | data formatting | bytes 12582912 | tf_op jit(solution)/shard_map/reshape | solution.py:34
  260.4 5.8 %fusion.3 = f32[768,192]{0,1:T(8,128)} fusion(bf16[768,4096]{1,0:T(8,128)(2,1)} %reshape.38, bf16[1,192,4096]{2,1,0:T(8,128)(2,1)S(1)} %copy-done.2), kind=kOutput, calls=%fused_computation.6 | convolution fusion | flops 1207959552 | bytes 8454144 | tf_op jit(solution)/shard_map/dot_general | solution.py:35
  266.3 13.5 %convolution_convert_fusion.1 = bf16[768,4096]{1,0:T(8,128)(2,1)} fusion(bf16[1,192,4096]{2,1,0:T(8,128)(2,1)S(1)} %copy-done, bf16[768,4096]{1,0:T(8,128)(2,1)} %reshape.38, bf16[1,192,4096]{2,1,0:T(8,128)(2,1)} %param.8, f32[768,192]{0,1:T(8,128)} %fusion.3), kind=kOutput, calls=%fused_computation.1 | convolution fusion | flops 2419949568 | bytes 16318464 | tf_op jit(solution)/shard_map/dot_general | solution.py:42
  279.7 9.8 %reshape.39 = bf16[64,12,4096]{2,1,0:T(8,128)(2,1)} reshape(bf16[768,4096]{1,0:T(8,128)(2,1)} %convolution_convert_fusion.1) | data formatting | bytes 12582912 | tf_op jit(solution)/shard_map/reshape | solution.py:44
  289.5 8.0 %all-to-all-start.1 = ((bf16[64,12,4096]{2,1,0:T(8,128)(2,1)}), bf16[64,12,4096]{2,1,0:T(8,128)(2,1)}, u32[]{:S(2)}, u32[]{:S(2)}) async-start(bf16[64,12,4096]{2,1,0:T(8,128)(2,1)} %reshape.39), calls=%async_computation.1 | async-start | bytes 16777216 | tf_op jit(solution)/shard_map/all_to_all | solution.py:43
  297.6 0.1 copy.26
  297.7 0.6 select_reduce_fusion
  298.3 183.5 %all-to-all-done.1 = bf16[64,12,4096]{2,1,0:T(8,128)(2,1)} async-done(((bf16[64,12,4096]{2,1,0:T(8,128)(2,1)}), bf16[64,12,4096]{2,1,0:T(8,128)(2,1)}, u32[]{:S(2)}, u32[]{:S(2)}) %all-to-all-start.1) | async-done | bytes 6291488 | tf_op jit(solution)/shard_map/all_to_all | solution.py:43
  481.8 9.9 %reshape.40 = bf16[768,4096]{1,0:T(8,128)(2,1)} reshape(bf16[64,12,4096]{2,1,0:T(8,128)(2,1)} %all-to-all-done.1) | data formatting | bytes 12582912 | tf_op jit(solution)/shard_map/reshape | solution.py:51
  491.6 4.8 convolution_convert_fusion.2
  496.5 36.9 %reduce-scatter.2.cloned.1.call-done = bf16[64,512]{1,0:T(8,128)(2,1)} async-done(((bf16[64,4096]{1,0:T(8,128)(2,1)}), bf16[64,512]{1,0:T(8,128)(2,1)}) %reduce-scatter.2.cloned.1.call-update) | async-done | bytes 65552 | tf_op jit(solution)/shard_map/reduce_scatter | solution.py:53
  (13 shorter events, 0.3 us)
Async XLA Ops:
  6.5 259.7 %copy-start = (bf16[1,192,4096]{2,1,0:T(8,128)(2,1)S(1)}, bf16[1,192,4096]{2,1,0:T(8,128)(2,1)}, u32[]{:S(2)}) copy-start(bf16[1,192,4096]{2,1,0:T(8,128)(2,1)} %param.9) | copy-start | bytes 4718596
  250.3 10.1 %copy-start.2 = (bf16[1,192,4096]{2,1,0:T(8,128)(2,1)S(1)}, bf16[1,192,4096]{2,1,0:T(8,128)(2,1)}, u32[]{:S(2)}) copy-start(bf16[1,192,4096]{2,1,0:T(8,128)(2,1)} %param.7) | copy-start | bytes 4718596
  289.5 8.1 %copy-start.1 = (bf16[64,8]{0,1:T(8,128)(2,1)S(1)}, bf16[64,8]{0,1:T(8,128)(2,1)}, u32[]{:S(2)}) copy-start(bf16[64,8]{0,1:T(8,128)(2,1)} %param.11) | copy-start | bytes 3076
  289.5 192.3 %all-to-all-start.1 = ((bf16[64,12,4096]{2,1,0:T(8,128)(2,1)}), bf16[64,12,4096]{2,1,0:T(8,128)(2,1)}, u32[]{:S(2)}, u32[]{:S(2)}) async-start(bf16[64,12,4096]{2,1,0:T(8,128)(2,1)} %reshape.39), calls=%async_computation.1 | async-start | bytes 16777216 | tf_op jit(solution)/shard_map/all_to_all | solution.py:43
  297.6 235.8 %reduce-scatter.2.cloned.1.call-start = ((), (), s32[]{:S(2)}) async-start(), calls=%async_computation.3 | async-start | bytes 589824 | tf_op jit(solution)/shard_map/reduce_scatter | solution.py:53
Sparse Core Ops, SparseCore 0:
  496.6 36.7 reduce-scatter.1
where the time goes:
time: 541 us; the launch traced here: 540 us
  blocking collectives  225 us (42%)
  waiting for transfers between devices  220 us (41%)
  local copies, waits for them, and re-layouts  41.1 us (8%)
  matrix products  28.6 us (5%)
  between operations  13.5 us (2%)
  starting transfers between devices  8.08 us (1%)
    all_to_all x1, blocking collectives, per_device(): lax.all_to_all(placed.astype(jnp.bfloat16).reshape(experts, capacity, who...  198 us
    all_to_all x1, waiting for transfers between devices, per_device(): lax.all_to_all(partial_value.astype(jnp.bfloat16).reshape(arrived.shape),...  184 us
    reduce_scatter x1, waiting for transfers between devices, per_device(): lax.psum_scatter(combined.astype(jnp.bfloat16), 'group', scatter_dimensio...  36.9 us
    all_gather x1, blocking collectives, per_device(): whole_rows = lax.all_gather(tokens, 'group', axis=1, tiled=True)  27.1 us
    dot_general x1, matrix products, per_device(): jnp.dot(hidden, down_weight[0], preferred_element_type=jnp.float32)  13.5 us
  transfers between devices with their start and end apart: 2, of which 2 were waited for; matrix products, arithmetic and copies ran while one was open for 0% of the time, Pallas kernels for 0%

commit v1 on v0

--- a/solution.py
+++ b/solution.py
@@ -20,7 +20,9 @@
     weights = jnp.sum(
         jnp.where(matches, gate_scores[:, :, None].astype(jnp.float32), 0.0), axis=1
     ).astype(jnp.bfloat16)
-    whole_rows = lax.all_gather(tokens, "group", axis=1, tiled=True)
+    whole_rows = jnp.concatenate(
+        lax.all_to_all(jnp.stack([tokens] * lax.axis_size("group")), "group", 0, 0), axis=1
+    )
     placed = lax.dot_general(
         selector, whole_rows, (((0,), (0,)), ((), ())), preferred_element_type=jnp.float32
     )

time: 541 us -> 532 us (0.983)
  blocking collectives: 225 us -> 198 us
  waiting for transfers between devices: 220 us -> 230 us
  starting transfers between devices: 8.08 us -> 15.2 us
    all_gather x1 -> x0, blocking collectives: 27.1 us -> none  [per_device(): whole_rows = lax.all_gather(tokens, 'group', axis=1, tiled=True)]
    all_to_all x0 -> x1, waiting for transfers between devices: none -> 13.4 us  [per_device(): lax.all_to_all(jnp.stack([tokens] * lax.axis_size('group')), 'group', 0, 0)]
    all_to_all x0 -> x1, starting transfers between devices: none -> 7.1 us  [per_device(): lax.all_to_all(jnp.stack([tokens] * lax.axis_size('group')), 'group', 0, 0)]
  transfers between devices with their start and end apart: 2 -> 3, of which waited for: 2 -> 3; matrix products, arithmetic and copies ran while one was open for 0% -> 1% of each run, Pallas kernels for 0% -> 0%
where the time goes in v1:
time: 532 us; the launch traced here: 531 us
  waiting for transfers between devices  230 us (43%)
  blocking collectives  198 us (37%)
  local copies, waits for them, and re-layouts  42.7 us (8%)
  matrix products  28 us (5%)
  starting transfers between devices  15.2 us (3%)
  between operations  13.5 us (3%)
    all_to_all x1, blocking collectives, per_device(): lax.all_to_all(placed.astype(jnp.bfloat16).reshape(experts, capacity, who...  198 us
    all_to_all x1, waiting for transfers between devices, per_device(): lax.all_to_all(partial_value.astype(jnp.bfloat16).reshape(arrived.shape),...  184 us
    reduce_scatter x1, waiting for transfers between devices, per_device(): lax.psum_scatter(combined.astype(jnp.bfloat16), 'group', scatter_dimensio...  33 us
    all_to_all x1, waiting for transfers between devices, per_device(): lax.all_to_all(jnp.stack([tokens] * lax.axis_size('group')), 'group', 0, 0)  13.4 us
    dot_general x1, matrix products, per_device(): jnp.dot(hidden, down_weight[0], preferred_element_type=jnp.float32)  13.3 us
  transfers between devices with their start and end apart: 3, of which 3 were waited for; matrix products, arithmetic and copies ran while one was open for 1% of the time, Pallas kernels for 0%

profile of v1, /device:TPU:2, one launch (start us, length us, event | category | flops | bytes accessed | tf_op | source)
XLA Modules:
  0.0 530.7 jit_solution(7177577532529289477)
XLA Ops:
  6.5 1.8 stack.2
  8.3 7.1 %all-to-all-start = ((bf16[8,64,512]{2,1,0:T(8,128)(2,1)}), bf16[8,64,512]{2,1,0:T(8,128)(2,1)S(1)}, u32[]{:S(2)}, u32[]{:S(2)}) async-start(bf16[8,64,512]{2,1,0:T(8,128)(2,1)} %stack.2), calls=%async_computation | async-start | bytes 1048576 | tf_op jit(solution)/shard_map/all_to_all | solution.py:24
  15.4 0.8 copy.29
  16.2 0.1 eq.42
  16.4 1.2 reduce-window.6
  17.6 0.2 slice_reduce_fusion
  17.9 0.1 fusion.22
  18.2 0.7 multiply_add_fusion
  19.0 0.5 fusion.5
  19.5 13.4 %all-to-all-done = bf16[8,64,512]{2,1,0:T(8,128)(2,1)S(1)} async-done(((bf16[8,64,512]{2,1,0:T(8,128)(2,1)}), bf16[8,64,512]{2,1,0:T(8,128)(2,1)S(1)}, u32[]{:S(2)}, u32[]{:S(2)}) %all-to-all-start) | async-done | bytes 524320 | tf_op jit(solution)/shard_map/all_to_all | solution.py:24
  33.0 4.6 convolution_convert_fusion
  37.5 9.8 %reshape.47 = bf16[64,12,4096]{2,1,0:T(8,128)(2,1)} reshape(bf16[768,4096]{1,0:T(8,128)(2,1)} %convolution_convert_fusion) | data formatting | bytes 12582912 | tf_op jit(solution)/shard_map/reshape | solution.py:30
  47.3 198.1 %all_to_all.15 = bf16[64,12,4096]{2,1,0:T(8,128)(2,1)} all-to-all(bf16[64,12,4096]{2,1,0:T(8,128)(2,1)} %reshape.47), channel_id=1, replica_groups=mesh['expert'=64,'group'=8] {'expert'}, dimensions={0} | all-to-all | bytes 12582912 | tf_op jit(solution)/shard_map/all_to_all | solution.py:29
  245.4 10.0 %reshape.48 = bf16[768,4096]{1,0:T(8,128)(2,1)} reshape(bf16[64,12,4096]{2,1,0:T(8,128)(2,1)} %all_to_all.15) | data formatting | bytes 12582912 | tf_op jit(solution)/shard_map/reshape | solution.py:36
  255.4 5.4 %fusion.3 = f32[768,192]{0,1:T(8,128)S(1)} fusion(bf16[768,4096]{1,0:T(8,128)(2,1)} %reshape.48, bf16[1,192,4096]{2,1,0:T(8,128)(2,1)} %param.7), kind=kOutput, calls=%fused_computation.6 | convolution fusion | flops 1207959552 | bytes 8454144 | tf_op jit(solution)/shard_map/dot_general | solution.py:37
  260.8 13.3 %convolution_convert_fusion.1 = bf16[768,4096]{1,0:T(8,128)(2,1)} fusion(bf16[1,192,4096]{2,1,0:T(8,128)(2,1)S(1)} %copy-done, bf16[768,4096]{1,0:T(8,128)(2,1)} %reshape.48, bf16[1,192,4096]{2,1,0:T(8,128)(2,1)} %param.8, f32[768,192]{0,1:T(8,128)S(1)} %fusion.3), kind=kOutput, calls=%fused_computation.1 | convolution fusion | flops 2419949568 | bytes 16318464 | tf_op jit(solution)/shard_map/dot_general | solution.py:44
  274.1 9.7 %reshape.49 = bf16[64,12,4096]{2,1,0:T(8,128)(2,1)} reshape(bf16[768,4096]{1,0:T(8,128)(2,1)} %convolution_convert_fusion.1) | data formatting | bytes 12582912 | tf_op jit(solution)/shard_map/reshape | solution.py:46
  283.9 8.1 %all-to-all-start.2 = ((bf16[64,12,4096]{2,1,0:T(8,128)(2,1)}), bf16[64,12,4096]{2,1,0:T(8,128)(2,1)}, u32[]{:S(2)}, u32[]{:S(2)}) async-start(bf16[64,12,4096]{2,1,0:T(8,128)(2,1)} %reshape.49), calls=%async_computation.2 | async-start | bytes 16777216 | tf_op jit(solution)/shard_map/all_to_all | solution.py:45
  292.0 0.1 copy.34
  292.1 0.6 select_reduce_fusion
  292.6 183.5 %all-to-all-done.2 = bf16[64,12,4096]{2,1,0:T(8,128)(2,1)} async-done(((bf16[64,12,4096]{2,1,0:T(8,128)(2,1)}), bf16[64,12,4096]{2,1,0:T(8,128)(2,1)}, u32[]{:S(2)}, u32[]{:S(2)}) %all-to-all-start.2) | async-done | bytes 6291488 | tf_op jit(solution)/shard_map/all_to_all | solution.py:45
  476.2 9.9 %reshape.50 = bf16[768,4096]{1,0:T(8,128)(2,1)} reshape(bf16[64,12,4096]{2,1,0:T(8,128)(2,1)} %all-to-all-done.2) | data formatting | bytes 12582912 | tf_op jit(solution)/shard_map/reshape | solution.py:53
  486.0 4.8 convolution_convert_fusion.2
  490.8 33.0 %reduce-scatter.2.cloned.1.call-done = bf16[64,512]{1,0:T(8,128)(2,1)} async-done(((bf16[64,4096]{1,0:T(8,128)(2,1)}), bf16[64,512]{1,0:T(8,128)(2,1)}) %reduce-scatter.2.cloned.1.call-update) | async-done | bytes 65552 | tf_op jit(solution)/shard_map/reduce_scatter | solution.py:55
  (14 shorter events, 0.5 us)
Async XLA Ops:
  6.5 254.3 %copy-start = (bf16[1,192,4096]{2,1,0:T(8,128)(2,1)S(1)}, bf16[1,192,4096]{2,1,0:T(8,128)(2,1)}, u32[]{:S(2)}) copy-start(bf16[1,192,4096]{2,1,0:T(8,128)(2,1)} %param.9) | copy-start | bytes 4718596
  8.3 24.6 %all-to-all-start = ((bf16[8,64,512]{2,1,0:T(8,128)(2,1)}), bf16[8,64,512]{2,1,0:T(8,128)(2,1)S(1)}, u32[]{:S(2)}, u32[]{:S(2)}) async-start(bf16[8,64,512]{2,1,0:T(8,128)(2,1)} %stack.2), calls=%async_computation | async-start | bytes 1048576 | tf_op jit(solution)/shard_map/all_to_all | solution.py:24
  283.8 8.1 %copy-start.1 = (bf16[64,8]{0,1:T(8,128)(2,1)S(1)}, bf16[64,8]{0,1:T(8,128)(2,1)}, u32[]{:S(2)}) copy-start(bf16[64,8]{0,1:T(8,128)(2,1)} %param.11) | copy-start | bytes 3076
  283.9 192.3 %all-to-all-start.2 = ((bf16[64,12,4096]{2,1,0:T(8,128)(2,1)}), bf16[64,12,4096]{2,1,0:T(8,128)(2,1)}, u32[]{:S(2)}, u32[]{:S(2)}) async-start(bf16[64,12,4096]{2,1,0:T(8,128)(2,1)} %reshape.49), calls=%async_computation.2 | async-start | bytes 16777216 | tf_op jit(solution)/shard_map/all_to_all | solution.py:45
  291.9 231.9 %reduce-scatter.2.cloned.1.call-start = ((), (), s32[]{:S(2)}) async-start(), calls=%async_computation.4 | async-start | bytes 589824 | tf_op jit(solution)/shard_map/reduce_scatter | solution.py:55
Sparse Core Ops, SparseCore 0:
  490.9 32.8 reduce-scatter.1
